TPU v7x, 256 devices: a whole 4x4x8 slice. The times are simulated.
256 devices in a mesh: section: 8 (over x, core), expert: 32 (over z, y).
Axes of the slice: x: 4, y: 4, z: 8, core: 2. Of those that a mesh axis runs over, the one named last changes fastest.
Arguments:
- tokens: bfloat16 [8, 2304, 2048], P(None, 'expert'), may hold values from -6 to 6
- w_in: bfloat16 [8, 2048, 2048], P('section', 'expert'), may hold values from -0.125 to 0.125
- w_out: bfloat16 [8, 2048, 2048], P('section', 'expert'), may hold values from -0.125 to 0.125
- router: bfloat16 [2048, 32], replicated, may hold values from -0.125 to 0.125
- exp_in: bfloat16 [32, 2048, 2048], P('expert', None, 'section'), may hold values from -0.125 to 0.125
- exp_out: bfloat16 [32, 2048, 2048], P('expert', 'section'), may hold values from -0.375 to 0.375
- active_rows: int32 [4608], P('expert'), may hold values from 0 to 575, as said below
- active_expert: int32 [4608, 1], P('expert'), may hold values from 0 to 31; in each aligned block of 144 rows (0 to 143, 144 to 287, ...) at most 13 rows name the same one
Outputs:
- updated: bfloat16 [8, 2304, 2048], P(None, 'expert', 'section')
Inputs may be any that keep to these rules, and one draw needn't show every extreme that they name: `active_rows`: the 144 entries of one token block name distinct rows of its 576 rows. `active_expert`: among the 144 entries of one token block no expert is named more than 13 times.
All inputs are finite; a program needn't handle non-finite values.
Results may differ from a plain program's by a relative error of at most 0.024.
Values may be sent and summed in bfloat16 or wider, within the bound.
No kernel may reach another device: no remote copies, remote signals or barrier semaphores. Data moves between devices by JAX's collectives and lax.ppermute only.
A program may use at most 64 MiB of HBM per device.

v0:
```python
import jax
import jax.numpy as jnp
from jax import lax
from jax.sharding import PartitionSpec as P


def from_behind(value, axis, steps):
    count = lax.axis_size(axis)
    initial, last = (max(0, -steps), min(count, count - steps))
    return lax.ppermute(value, axis, [(source, source + steps) for source in range(initial, last)])


def spread(shard, axis, root):
    mine = lax.axis_index(axis) == root
    return lax.psum(jnp.where(mine, shard, jnp.zeros_like(shard)), axis)


def normalize(rows):
    wide = rows.astype(jnp.float32)
    scale = lax.rsqrt(jnp.mean(wide * wide, axis=-1, keepdims=True) + 1e-05)
    return wide * scale


def processor(stream, w_first, w_second):
    normed = normalize(stream).astype(jnp.bfloat16)
    hidden = jax.nn.silu(jnp.dot(normed, w_first, preferred_element_type=jnp.float32)).astype(
        jnp.bfloat16
    )
    branch = jnp.dot(hidden, w_second, preferred_element_type=jnp.float32)
    return (stream.astype(jnp.float32) + branch).astype(jnp.bfloat16)


def local(tokens, w_in, w_out, router, exp_in, exp_out, active_rows, active_expert):
    n_section = lax.axis_size("section")
    section = lax.axis_index("section")
    micro, tok_dev, width = tokens.shape
    w_first, w_second = (
        lax.all_gather(w_in, "expert", axis=1, tiled=True),
        lax.all_gather(w_out, "expert", axis=1, tiled=True),
    )
    w_first = w_first[0]
    w_second = w_second[0]
    last = n_section - 1

    def run_layer(stream):
        return processor(stream, w_first, w_second)

    def skip_layer(stream):
        return jnp.zeros_like(stream)

    def tick(step, carry):
        incoming, collected = carry
        micro_index = step - section
        valid = (micro_index >= 0) & (micro_index < micro)
        clamped = jnp.clip(micro_index, 0, micro - 1)
        fresh = lax.dynamic_index_in_dim(tokens, clamped, 0, keepdims=False)
        stream = jnp.where(section == 0, fresh, incoming)
        result = lax.cond(valid, run_layer, skip_layer, stream)
        updated = lax.dynamic_update_index_in_dim(collected, result, clamped, 0)
        collected = jnp.where(valid & (section == last), updated, collected)
        passed = from_behind(result, "section", 1)
        return (passed, collected)

    start = (jnp.zeros((tok_dev, width), jnp.bfloat16), jnp.zeros_like(tokens))
    passed, collected = lax.fori_loop(0, micro + n_section - 1, tick, start)
    final = spread(collected, "section", last)
    rows_dev = micro * tok_dev
    flat = final.reshape(rows_dev, width)
    n_exp = router.shape[1]
    act_dev = active_rows.shape[0]
    capacity = 3 * act_dev // n_exp
    picked = jnp.take(flat, active_rows, axis=0)
    contact = normalize(picked).astype(jnp.bfloat16)
    chosen = active_expert[:, 0]
    onehot = chosen[:, None] == jnp.arange(n_exp, dtype=jnp.int32)[None, :]
    logits = jnp.dot(contact, router, preferred_element_type=jnp.float32)
    gate = jax.nn.sigmoid(jnp.sum(jnp.where(onehot, logits, 0.0), axis=1))
    counts = onehot.astype(jnp.int32)
    earlier = jnp.cumsum(counts, axis=0) - counts
    rank = jnp.sum(earlier * counts, axis=1)
    position = chosen * capacity + rank
    placing = (jnp.arange(n_exp * capacity, dtype=jnp.int32)[:, None] == position[None, :]).astype(
        jnp.bfloat16
    )
    outgoing = jnp.dot(placing, contact, preferred_element_type=jnp.float32).astype(jnp.bfloat16)
    outgoing = outgoing.reshape(n_exp, capacity, width)
    e_first = exp_in[0]
    e_second = exp_out[0]
    arrived = lax.all_to_all(outgoing, "expert", split_axis=0, concat_axis=0, tiled=True)
    sources, slots, _ = arrived.shape
    rows = arrived.reshape(sources * slots, width)
    hidden = jax.nn.silu(jnp.dot(rows, e_first, preferred_element_type=jnp.float32)).astype(
        jnp.bfloat16
    )
    partial_value = jnp.dot(hidden, e_second, preferred_element_type=jnp.float32).reshape(
        sources, slots, width
    )
    part_width = width // n_section
    returned = lax.all_to_all(
        partial_value.astype(jnp.bfloat16), "expert", split_axis=0, concat_axis=0, tiled=True
    ).astype(partial_value.dtype)
    mine = jnp.take(returned.reshape(n_exp * capacity, width), position, axis=0)
    added = lax.psum_scatter(
        (gate[:, None] * mine).astype(jnp.bfloat16), "section", scatter_dimension=1, tiled=True
    ).astype(jnp.float32)
    base = lax.dynamic_slice_in_dim(flat, section * part_width, part_width, 1).astype(jnp.float32)
    mixed = base.at[active_rows].add(added)
    return mixed.astype(jnp.bfloat16).reshape(micro, tok_dev, part_width)


def solution(mesh):
    return jax.shard_map(
        local,
        mesh=mesh,
        in_specs=(
            P(None, "expert", None),
            P("section", "expert", None),
            P("section", "expert", None),
            P(),
            P("expert", None, "section"),
            P("expert", "section", None),
            P("expert"),
            P("expert", None),
        ),
        out_specs=P(None, "expert", "section"),
        check_vma=False,
    )
```

profile of v0, /device:TPU:8, one launch (start us, length us, event | category | flops | bytes accessed | tf_op | source)
XLA Modules:
  0.0 731.9 jit_solution(625709644638391980)
XLA Ops:
  9.4 100.1 %all-gather.3.cloned.1.call-done = bf16[1,2048,2048]{2,1,0:T(8,128)(2,1)} async-done(((bf16[1,64,2048]{2,1,0:T(8,128)(2,1)}), bf16[1,2048,2048]{2,1,0:T(8,128)(2,1)}) %all-gather.3.cloned.1.call-update) | async-done | bytes 8388624 | tf_op jit(solution)/shard_map/all_gather | solution.py:38
  109.4 97.6 %all-gather.5.cloned.1.call-done = bf16[1,2048,2048]{2,1,0:T(8,128)(2,1)} async-done(((bf16[1,64,2048]{2,1,0:T(8,128)(2,1)}), bf16[1,2048,2048]{2,1,0:T(8,128)(2,1)}) %all-gather.5.cloned.1.call-update) | async-done | bytes 8388624 | tf_op jit(solution)/shard_map/all_gather | solution.py:39
  207.0 1.7 broadcast.91
  208.8 244.6 %while.16 = (s32[]{:T(128)}, bf16[72,2048]{1,0:T(8,128)(2,1)S(1)}, bf16[8,72,2048]{2,1,0:T(8,128)(2,1)}, s32[]{:T(128)}, pred[]{:T(512)}, /*index=5*/bf16[8,72,2...) while((s32[]{:T(128)}, bf16[72,2048]{1,0:T(8,128)(2,1)S(1)}, ...), condition=%wide.region_4.5_spmd, body=%wide.region_0.4_spmd.sunk | while | flops 1210613888 | bytes 21500040 | solution.py:65
  208.8 11.9 %conditional.2 = (bf16[72,2048]{1,0:T(8,128)(2,1)}, bf16[1,72,2048]{2,1,0:T(8,128)(2,1)S(1)}) conditional(s32[]{:T(128)} %convert_element_type.109, () %tuple.47, (pred[]{:T(512)}, bf16[8,72,2048]{2,1,0:T(8,128)(2,1)}, s32[]{:T(128)}, bf16[72,2048]{1,0:T(8,128)(2,1)S(1)}, bf16[2048,2048]{1,0:T(8,128)(2,1)}, ...), branch_computations={%region_1.1_spmd, %region_2.3_spmd} | conditional | flops 1210466432 | bytes 19434868 | solution.py:58
  210.0 9.7 %fusion = bf16[72,2048]{1,0:T(8,128)(2,1)} fusion(bf16[2048,2048]{1,0:T(8,128)(2,1)} %get-tuple-element.195, bf16[2048,2048]{1,0:T(8,128)(2,1)} %get-tuple-element.194, f32[72]{0:T(128)S(1)} %add_rsqrt_fusion, bf16[72,2048]{1,0:T(8,128)(2,1)S(1)} %get-tuple-element.193, bf16[8,72,2048]{2,1,0:T(8,128)(2,1)} %get-tuple-element.191, s32[]{:T(128)} %get-tuple-element.192, ...), kind=kOutput, calls=%fused_computation.4 | convolution fusion | flops 1209876480 | bytes 18254336 | tf_op jit(solution)/shard_map/while/body/eval_jaxpr/cond/branch_1_fun/dot_general | solution.py:29
  222.0 1.7 select_dynamic-update-slice_fusion.2
  223.7 11.9 %conditional.2 = (bf16[72,2048]{1,0:T(8,128)(2,1)}, bf16[1,72,2048]{2,1,0:T(8,128)(2,1)S(1)}) conditional(s32[]{:T(128)} %convert_element_type.109, () %tuple.47, (pred[]{:T(512)}, bf16[8,72,2048]{2,1,0:T(8,128)(2,1)}, s32[]{:T(128)}, bf16[72,2048]{1,0:T(8,128)(2,1)S(1)}, bf16[2048,2048]{1,0:T(8,128)(2,1)}, ...), branch_computations={%region_1.1_spmd, %region_2.3_spmd} | conditional | flops 1210466432 | bytes 19434868 | solution.py:58
  224.9 9.7 %fusion = bf16[72,2048]{1,0:T(8,128)(2,1)} fusion(bf16[2048,2048]{1,0:T(8,128)(2,1)} %get-tuple-element.195, bf16[2048,2048]{1,0:T(8,128)(2,1)} %get-tuple-element.194, f32[72]{0:T(128)S(1)} %add_rsqrt_fusion, bf16[72,2048]{1,0:T(8,128)(2,1)S(1)} %get-tuple-element.193, bf16[8,72,2048]{2,1,0:T(8,128)(2,1)} %get-tuple-element.191, s32[]{:T(128)} %get-tuple-element.192, ...), kind=kOutput, calls=%fused_computation.4 | convolution fusion | flops 1209876480 | bytes 18254336 | tf_op jit(solution)/shard_map/while/body/eval_jaxpr/cond/branch_1_fun/dot_general | solution.py:29
  235.6 1.9 collective-permute-start
  237.5 1.7 select_dynamic-update-slice_fusion.2
  239.2 11.9 %conditional.2 = (bf16[72,2048]{1,0:T(8,128)(2,1)}, bf16[1,72,2048]{2,1,0:T(8,128)(2,1)S(1)}) conditional(s32[]{:T(128)} %convert_element_type.109, () %tuple.47, (pred[]{:T(512)}, bf16[8,72,2048]{2,1,0:T(8,128)(2,1)}, s32[]{:T(128)}, bf16[72,2048]{1,0:T(8,128)(2,1)S(1)}, bf16[2048,2048]{1,0:T(8,128)(2,1)}, ...), branch_computations={%region_1.1_spmd, %region_2.3_spmd} | conditional | flops 1210466432 | bytes 19434868 | solution.py:58
  240.4 9.7 %fusion = bf16[72,2048]{1,0:T(8,128)(2,1)} fusion(bf16[2048,2048]{1,0:T(8,128)(2,1)} %get-tuple-element.195, bf16[2048,2048]{1,0:T(8,128)(2,1)} %get-tuple-element.194, f32[72]{0:T(128)S(1)} %add_rsqrt_fusion, bf16[72,2048]{1,0:T(8,128)(2,1)S(1)} %get-tuple-element.193, bf16[8,72,2048]{2,1,0:T(8,128)(2,1)} %get-tuple-element.191, s32[]{:T(128)} %get-tuple-element.192, ...), kind=kOutput, calls=%fused_computation.4 | convolution fusion | flops 1209876480 | bytes 18254336 | tf_op jit(solution)/shard_map/while/body/eval_jaxpr/cond/branch_1_fun/dot_general | solution.py:29
  251.1 4.1 collective-permute-start
  255.2 1.7 select_dynamic-update-slice_fusion.2
  257.0 11.8 %conditional.2 = (bf16[72,2048]{1,0:T(8,128)(2,1)}, bf16[1,72,2048]{2,1,0:T(8,128)(2,1)S(1)}) conditional(s32[]{:T(128)} %convert_element_type.109, () %tuple.47, (pred[]{:T(512)}, bf16[8,72,2048]{2,1,0:T(8,128)(2,1)}, s32[]{:T(128)}, bf16[72,2048]{1,0:T(8,128)(2,1)S(1)}, bf16[2048,2048]{1,0:T(8,128)(2,1)}, ...), branch_computations={%region_1.1_spmd, %region_2.3_spmd} | conditional | flops 1210466432 | bytes 19434868 | solution.py:58
  258.1 9.7 %fusion = bf16[72,2048]{1,0:T(8,128)(2,1)} fusion(bf16[2048,2048]{1,0:T(8,128)(2,1)} %get-tuple-element.195, bf16[2048,2048]{1,0:T(8,128)(2,1)} %get-tuple-element.194, f32[72]{0:T(128)S(1)} %add_rsqrt_fusion, bf16[72,2048]{1,0:T(8,128)(2,1)S(1)} %get-tuple-element.193, bf16[8,72,2048]{2,1,0:T(8,128)(2,1)} %get-tuple-element.191, s32[]{:T(128)} %get-tuple-element.192, ...), kind=kOutput, calls=%fused_computation.4 | convolution fusion | flops 1209876480 | bytes 18254336 | tf_op jit(solution)/shard_map/while/body/eval_jaxpr/cond/branch_1_fun/dot_general | solution.py:29
  268.8 6.5 collective-permute-start
  275.3 1.7 select_dynamic-update-slice_fusion.2
  277.0 11.8 %conditional.2 = (bf16[72,2048]{1,0:T(8,128)(2,1)}, bf16[1,72,2048]{2,1,0:T(8,128)(2,1)S(1)}) conditional(s32[]{:T(128)} %convert_element_type.109, () %tuple.47, (pred[]{:T(512)}, bf16[8,72,2048]{2,1,0:T(8,128)(2,1)}, s32[]{:T(128)}, bf16[72,2048]{1,0:T(8,128)(2,1)S(1)}, bf16[2048,2048]{1,0:T(8,128)(2,1)}, ...), branch_computations={%region_1.1_spmd, %region_2.3_spmd} | conditional | flops 1210466432 | bytes 19434868 | solution.py:58
  278.2 9.7 %fusion = bf16[72,2048]{1,0:T(8,128)(2,1)} fusion(bf16[2048,2048]{1,0:T(8,128)(2,1)} %get-tuple-element.195, bf16[2048,2048]{1,0:T(8,128)(2,1)} %get-tuple-element.194, f32[72]{0:T(128)S(1)} %add_rsqrt_fusion, bf16[72,2048]{1,0:T(8,128)(2,1)S(1)} %get-tuple-element.193, bf16[8,72,2048]{2,1,0:T(8,128)(2,1)} %get-tuple-element.191, s32[]{:T(128)} %get-tuple-element.192, ...), kind=kOutput, calls=%fused_computation.4 | convolution fusion | flops 1209876480 | bytes 18254336 | tf_op jit(solution)/shard_map/while/body/eval_jaxpr/cond/branch_1_fun/dot_general | solution.py:29
  288.9 6.5 collective-permute-start
  295.4 1.8 select_dynamic-update-slice_fusion.2
  297.2 11.8 %conditional.2 = (bf16[72,2048]{1,0:T(8,128)(2,1)}, bf16[1,72,2048]{2,1,0:T(8,128)(2,1)S(1)}) conditional(s32[]{:T(128)} %convert_element_type.109, () %tuple.47, (pred[]{:T(512)}, bf16[8,72,2048]{2,1,0:T(8,128)(2,1)}, s32[]{:T(128)}, bf16[72,2048]{1,0:T(8,128)(2,1)S(1)}, bf16[2048,2048]{1,0:T(8,128)(2,1)}, ...), branch_computations={%region_1.1_spmd, %region_2.3_spmd} | conditional | flops 1210466432 | bytes 19434868 | solution.py:58
  298.3 9.7 %fusion = bf16[72,2048]{1,0:T(8,128)(2,1)} fusion(bf16[2048,2048]{1,0:T(8,128)(2,1)} %get-tuple-element.195, bf16[2048,2048]{1,0:T(8,128)(2,1)} %get-tuple-element.194, f32[72]{0:T(128)S(1)} %add_rsqrt_fusion, bf16[72,2048]{1,0:T(8,128)(2,1)S(1)} %get-tuple-element.193, bf16[8,72,2048]{2,1,0:T(8,128)(2,1)} %get-tuple-element.191, s32[]{:T(128)} %get-tuple-element.192, ...), kind=kOutput, calls=%fused_computation.4 | convolution fusion | flops 1209876480 | bytes 18254336 | tf_op jit(solution)/shard_map/while/body/eval_jaxpr/cond/branch_1_fun/dot_general | solution.py:29
  309.0 6.5 collective-permute-start
  315.5 1.8 select_dynamic-update-slice_fusion.2
  317.2 11.8 %conditional.2 = (bf16[72,2048]{1,0:T(8,128)(2,1)}, bf16[1,72,2048]{2,1,0:T(8,128)(2,1)S(1)}) conditional(s32[]{:T(128)} %convert_element_type.109, () %tuple.47, (pred[]{:T(512)}, bf16[8,72,2048]{2,1,0:T(8,128)(2,1)}, s32[]{:T(128)}, bf16[72,2048]{1,0:T(8,128)(2,1)S(1)}, bf16[2048,2048]{1,0:T(8,128)(2,1)}, ...), branch_computations={%region_1.1_spmd, %region_2.3_spmd} | conditional | flops 1210466432 | bytes 19434868 | solution.py:58
  318.4 9.7 %fusion = bf16[72,2048]{1,0:T(8,128)(2,1)} fusion(bf16[2048,2048]{1,0:T(8,128)(2,1)} %get-tuple-element.195, bf16[2048,2048]{1,0:T(8,128)(2,1)} %get-tuple-element.194, f32[72]{0:T(128)S(1)} %add_rsqrt_fusion, bf16[72,2048]{1,0:T(8,128)(2,1)S(1)} %get-tuple-element.193, bf16[8,72,2048]{2,1,0:T(8,128)(2,1)} %get-tuple-element.191, s32[]{:T(128)} %get-tuple-element.192, ...), kind=kOutput, calls=%fused_computation.4 | convolution fusion | flops 1209876480 | bytes 18254336 | tf_op jit(solution)/shard_map/while/body/eval_jaxpr/cond/branch_1_fun/dot_general | solution.py:29
  329.1 6.5 collective-permute-start
  335.6 1.8 select_dynamic-update-slice_fusion.2
  337.3 11.8 %conditional.2 = (bf16[72,2048]{1,0:T(8,128)(2,1)}, bf16[1,72,2048]{2,1,0:T(8,128)(2,1)S(1)}) conditional(s32[]{:T(128)} %convert_element_type.109, () %tuple.47, (pred[]{:T(512)}, bf16[8,72,2048]{2,1,0:T(8,128)(2,1)}, s32[]{:T(128)}, bf16[72,2048]{1,0:T(8,128)(2,1)S(1)}, bf16[2048,2048]{1,0:T(8,128)(2,1)}, ...), branch_computations={%region_1.1_spmd, %region_2.3_spmd} | conditional | flops 1210466432 | bytes 19434868 | solution.py:58
  338.5 9.7 %fusion = bf16[72,2048]{1,0:T(8,128)(2,1)} fusion(bf16[2048,2048]{1,0:T(8,128)(2,1)} %get-tuple-element.195, bf16[2048,2048]{1,0:T(8,128)(2,1)} %get-tuple-element.194, f32[72]{0:T(128)S(1)} %add_rsqrt_fusion, bf16[72,2048]{1,0:T(8,128)(2,1)S(1)} %get-tuple-element.193, bf16[8,72,2048]{2,1,0:T(8,128)(2,1)} %get-tuple-element.191, s32[]{:T(128)} %get-tuple-element.192, ...), kind=kOutput, calls=%fused_computation.4 | convolution fusion | flops 1209876480 | bytes 18254336 | tf_op jit(solution)/shard_map/while/body/eval_jaxpr/cond/branch_1_fun/dot_general | solution.py:29
  349.2 6.5 collective-permute-start
  355.7 1.8 select_dynamic-update-slice_fusion.2
  358.2 17.5 %collective-permute-start = (bf16[72,2048]{1,0:T(8,128)(2,1)}, bf16[72,2048]{1,0:T(8,128)(2,1)S(1)}, u32[]{:S(2)}, u32[]{:S(2)}) collective-permute-start(bf16[72,2048]{1,0:T(8,128)(2,1)} %get-tuple-element.287), channel_id=1, source_target_pairs={{0,32},{32,64},{64,96},{96,128},{128,160},{160,192},{192,224},{1,3... | collective-permute-start | bytes 884744 | tf_op jit(solution)/shard_map/while/body/eval_jaxpr/ppermute | solution.py:10
  375.8 1.8 select_dynamic-update-slice_fusion.2
  378.3 6.5 collective-permute-start
  384.8 1.8 select_dynamic-update-slice_fusion.2
  387.3 17.5 %collective-permute-start = (bf16[72,2048]{1,0:T(8,128)(2,1)}, bf16[72,2048]{1,0:T(8,128)(2,1)S(1)}, u32[]{:S(2)}, u32[]{:S(2)}) collective-permute-start(bf16[72,2048]{1,0:T(8,128)(2,1)} %get-tuple-element.287), channel_id=1, source_target_pairs={{0,32},{32,64},{64,96},{96,128},{128,160},{160,192},{192,224},{1,3... | collective-permute-start | bytes 884744 | tf_op jit(solution)/shard_map/while/body/eval_jaxpr/ppermute | solution.py:10
  404.9 1.8 select_dynamic-update-slice_fusion.2
  407.4 6.5 collective-permute-start
  413.9 1.8 select_dynamic-update-slice_fusion.2
  416.4 8.4 %collective-permute-start = (bf16[72,2048]{1,0:T(8,128)(2,1)}, bf16[72,2048]{1,0:T(8,128)(2,1)S(1)}, u32[]{:S(2)}, u32[]{:S(2)}) collective-permute-start(bf16[72,2048]{1,0:T(8,128)(2,1)} %get-tuple-element.287), channel_id=1, source_target_pairs={{0,32},{32,64},{64,96},{96,128},{128,160},{160,192},{192,224},{1,3... | collective-permute-start | bytes 884744 | tf_op jit(solution)/shard_map/while/body/eval_jaxpr/ppermute | solution.py:10
  424.9 1.8 select_dynamic-update-slice_fusion.2
  427.4 6.5 collective-permute-start
  433.9 1.8 select_dynamic-update-slice_fusion.2
  436.5 15.2 %collective-permute-start = (bf16[72,2048]{1,0:T(8,128)(2,1)}, bf16[72,2048]{1,0:T(8,128)(2,1)S(1)}, u32[]{:S(2)}, u32[]{:S(2)}) collective-permute-start(bf16[72,2048]{1,0:T(8,128)(2,1)} %get-tuple-element.287), channel_id=1, source_target_pairs={{0,32},{32,64},{64,96},{96,128},{128,160},{160,192},{192,224},{1,3... | collective-permute-start | bytes 884744 | tf_op jit(solution)/shard_map/while/body/eval_jaxpr/ppermute | solution.py:10
  451.6 1.8 select_dynamic-update-slice_fusion.2
  453.4 1.6 broadcast_select_fusion
  455.8 99.3 %all-reduce.3.cloned.1.call-done = bf16[576,2048]{1,0:T(8,128)(2,1)} async-done(((bf16[576,2048]{1,0:T(8,128)(2,1)}), bf16[576,2048]{1,0:T(8,128)(2,1)}) %all-reduce.3.cloned.1.call-update) | async-done | bytes 2359312 | tf_op jit(solution)/shard_map/psum | solution.py:15
  555.1 3.5 gather_fusion
  559.4 1.9 convolution_convert_fusion.1
  561.3 1.8 reshape.75
  563.1 58.7 %all_to_all.10 = bf16[32,13,2048]{2,1,0:T(8,128)(2,1)} all-to-all(bf16[32,13,2048]{2,1,0:T(8,128)(2,1)S(1)} %reshape.75), channel_id=1, replica_groups=mesh['section'=8,'expert'=32] {'expert'}, dimensions={0} | all-to-all | bytes 3407872 | tf_op jit(solution)/shard_map/all_to_all | solution.py:89
  621.8 1.8 reshape.76
  623.7 1.9 multiply_convert_fusion.3
  626.3 2.3 copy.18
  628.6 5.7 all-to-all-start.1
  635.8 46.3 %all-to-all-done.1 = bf16[32,13,2048]{2,1,0:T(8,128)(2,1)S(1)} async-done(((bf16[32,13,2048]{2,1,0:T(8,128)(2,1)}), bf16[32,13,2048]{2,1,0:T(8,128)(2,1)S(1)}, u32[]{:S(2)}, u32[]{:S(2)}) %all-to-all-start.1) | async-done | bytes 1703968 | tf_op jit(solution)/shard_map/all_to_all | solution.py:99
  682.1 2.0 reshape.82
  684.1 3.5 gather_fusion.1
  689.7 33.0 %reduce-scatter.2.cloned.1.call-done = bf16[144,256]{1,0:T(8,128)(2,1)} async-done(((bf16[144,2048]{1,0:T(8,128)(2,1)}), bf16[144,256]{1,0:T(8,128)(2,1)}) %reduce-scatter.2.cloned.1.call-update) | async-done | bytes 73744 | tf_op jit(solution)/shard_map/reduce_scatter | solution.py:103
  722.7 2.0 scatter_custom_fusion
  (103 shorter events, 38.5 us)
Async XLA Ops:
  6.5 619.1 %copy-start = (bf16[1,256,2048]{2,1,0:T(8,128)(2,1)S(1)}, bf16[1,256,2048]{2,1,0:T(8,128)(2,1)}, u32[]{:S(2)}) copy-start(bf16[1,256,2048]{2,1,0:T(8,128)(2,1)} %param.17) | copy-start | bytes 3145732
  6.5 102.9 %all-gather.3.cloned.1.call-start = ((), (), s32[]{:S(2)}) async-start(), calls=%async_computation.3 | async-start | bytes 8650752 | tf_op jit(solution)/shard_map/all_gather | solution.py:38
  7.3 199.8 %all-gather.5.cloned.1.call-start = ((), (), s32[]{:S(2)}) async-start(), calls=%async_computation.4 | async-start | bytes 8650752 | tf_op jit(solution)/shard_map/all_gather | solution.py:39
  8.0 547.0 %all-reduce.3.cloned.1.call-start = ((), (), s32[]{:S(2)}) async-start(), calls=%async_computation.5 | async-start | bytes 4718592 | tf_op jit(solution)/shard_map/psum | solution.py:15
  220.7 3.1 collective-permute-start
  235.6 3.7 collective-permute-start
  251.1 5.9 collective-permute-start
  268.8 8.2 %collective-permute-start = (bf16[72,2048]{1,0:T(8,128)(2,1)}, bf16[72,2048]{1,0:T(8,128)(2,1)S(1)}, u32[]{:S(2)}, u32[]{:S(2)}) collective-permute-start(bf16[72,2048]{1,0:T(8,128)(2,1)} %get-tuple-element.287), channel_id=1, source_target_pairs={{0,32},{32,64},{64,96},{96,128},{128,160},{160,192},{192,224},{1,3... | collective-permute-start | bytes 884744 | tf_op jit(solution)/shard_map/while/body/eval_jaxpr/ppermute | solution.py:10
  288.9 8.3 %collective-permute-start = (bf16[72,2048]{1,0:T(8,128)(2,1)}, bf16[72,2048]{1,0:T(8,128)(2,1)S(1)}, u32[]{:S(2)}, u32[]{:S(2)}) collective-permute-start(bf16[72,2048]{1,0:T(8,128)(2,1)} %get-tuple-element.287), channel_id=1, source_target_pairs={{0,32},{32,64},{64,96},{96,128},{128,160},{160,192},{192,224},{1,3... | collective-permute-start | bytes 884744 | tf_op jit(solution)/shard_map/while/body/eval_jaxpr/ppermute | solution.py:10
  309.0 8.2 %collective-permute-start = (bf16[72,2048]{1,0:T(8,128)(2,1)}, bf16[72,2048]{1,0:T(8,128)(2,1)S(1)}, u32[]{:S(2)}, u32[]{:S(2)}) collective-permute-start(bf16[72,2048]{1,0:T(8,128)(2,1)} %get-tuple-element.287), channel_id=1, source_target_pairs={{0,32},{32,64},{64,96},{96,128},{128,160},{160,192},{192,224},{1,3... | collective-permute-start | bytes 884744 | tf_op jit(solution)/shard_map/while/body/eval_jaxpr/ppermute | solution.py:10
  329.1 8.2 %collective-permute-start = (bf16[72,2048]{1,0:T(8,128)(2,1)}, bf16[72,2048]{1,0:T(8,128)(2,1)S(1)}, u32[]{:S(2)}, u32[]{:S(2)}) collective-permute-start(bf16[72,2048]{1,0:T(8,128)(2,1)} %get-tuple-element.287), channel_id=1, source_target_pairs={{0,32},{32,64},{64,96},{96,128},{128,160},{160,192},{192,224},{1,3... | collective-permute-start | bytes 884744 | tf_op jit(solution)/shard_map/while/body/eval_jaxpr/ppermute | solution.py:10
  349.2 8.2 %collective-permute-start = (bf16[72,2048]{1,0:T(8,128)(2,1)}, bf16[72,2048]{1,0:T(8,128)(2,1)S(1)}, u32[]{:S(2)}, u32[]{:S(2)}) collective-permute-start(bf16[72,2048]{1,0:T(8,128)(2,1)} %get-tuple-element.287), channel_id=1, source_target_pairs={{0,32},{32,64},{64,96},{96,128},{128,160},{160,192},{192,224},{1,3... | collective-permute-start | bytes 884744 | tf_op jit(solution)/shard_map/while/body/eval_jaxpr/ppermute | solution.py:10
  358.2 19.3 %collective-permute-start = (bf16[72,2048]{1,0:T(8,128)(2,1)}, bf16[72,2048]{1,0:T(8,128)(2,1)S(1)}, u32[]{:S(2)}, u32[]{:S(2)}) collective-permute-start(bf16[72,2048]{1,0:T(8,128)(2,1)} %get-tuple-element.287), channel_id=1, source_target_pairs={{0,32},{32,64},{64,96},{96,128},{128,160},{160,192},{192,224},{1,3... | collective-permute-start | bytes 884744 | tf_op jit(solution)/shard_map/while/body/eval_jaxpr/ppermute | solution.py:10
  378.3 8.3 %collective-permute-start = (bf16[72,2048]{1,0:T(8,128)(2,1)}, bf16[72,2048]{1,0:T(8,128)(2,1)S(1)}, u32[]{:S(2)}, u32[]{:S(2)}) collective-permute-start(bf16[72,2048]{1,0:T(8,128)(2,1)} %get-tuple-element.287), channel_id=1, source_target_pairs={{0,32},{32,64},{64,96},{96,128},{128,160},{160,192},{192,224},{1,3... | collective-permute-start | bytes 884744 | tf_op jit(solution)/shard_map/while/body/eval_jaxpr/ppermute | solution.py:10
  387.3 19.3 %collective-permute-start = (bf16[72,2048]{1,0:T(8,128)(2,1)}, bf16[72,2048]{1,0:T(8,128)(2,1)S(1)}, u32[]{:S(2)}, u32[]{:S(2)}) collective-permute-start(bf16[72,2048]{1,0:T(8,128)(2,1)} %get-tuple-element.287), channel_id=1, source_target_pairs={{0,32},{32,64},{64,96},{96,128},{128,160},{160,192},{192,224},{1,3... | collective-permute-start | bytes 884744 | tf_op jit(solution)/shard_map/while/body/eval_jaxpr/ppermute | solution.py:10
  407.4 8.3 %collective-permute-start = (bf16[72,2048]{1,0:T(8,128)(2,1)}, bf16[72,2048]{1,0:T(8,128)(2,1)S(1)}, u32[]{:S(2)}, u32[]{:S(2)}) collective-permute-start(bf16[72,2048]{1,0:T(8,128)(2,1)} %get-tuple-element.287), channel_id=1, source_target_pairs={{0,32},{32,64},{64,96},{96,128},{128,160},{160,192},{192,224},{1,3... | collective-permute-start | bytes 884744 | tf_op jit(solution)/shard_map/while/body/eval_jaxpr/ppermute | solution.py:10
  416.4 10.2 %collective-permute-start = (bf16[72,2048]{1,0:T(8,128)(2,1)}, bf16[72,2048]{1,0:T(8,128)(2,1)S(1)}, u32[]{:S(2)}, u32[]{:S(2)}) collective-permute-start(bf16[72,2048]{1,0:T(8,128)(2,1)} %get-tuple-element.287), channel_id=1, source_target_pairs={{0,32},{32,64},{64,96},{96,128},{128,160},{160,192},{192,224},{1,3... | collective-permute-start | bytes 884744 | tf_op jit(solution)/shard_map/while/body/eval_jaxpr/ppermute | solution.py:10
  427.4 8.3 %collective-permute-start = (bf16[72,2048]{1,0:T(8,128)(2,1)}, bf16[72,2048]{1,0:T(8,128)(2,1)S(1)}, u32[]{:S(2)}, u32[]{:S(2)}) collective-permute-start(bf16[72,2048]{1,0:T(8,128)(2,1)} %get-tuple-element.287), channel_id=1, source_target_pairs={{0,32},{32,64},{64,96},{96,128},{128,160},{160,192},{192,224},{1,3... | collective-permute-start | bytes 884744 | tf_op jit(solution)/shard_map/while/body/eval_jaxpr/ppermute | solution.py:10
  436.5 17.0 %collective-permute-start = (bf16[72,2048]{1,0:T(8,128)(2,1)}, bf16[72,2048]{1,0:T(8,128)(2,1)S(1)}, u32[]{:S(2)}, u32[]{:S(2)}) collective-permute-start(bf16[72,2048]{1,0:T(8,128)(2,1)} %get-tuple-element.287), channel_id=1, source_target_pairs={{0,32},{32,64},{64,96},{96,128},{128,160},{160,192},{192,224},{1,3... | collective-permute-start | bytes 884744 | tf_op jit(solution)/shard_map/while/body/eval_jaxpr/ppermute | solution.py:10
  455.0 0.7 copy-start.3
  455.0 0.8 copy-start.2
  558.6 0.8 copy-start.1
  628.6 5.8 copy-start.4
  628.6 53.6 %all-to-all-start.1 = ((bf16[32,13,2048]{2,1,0:T(8,128)(2,1)}), bf16[32,13,2048]{2,1,0:T(8,128)(2,1)S(1)}, u32[]{:S(2)}, u32[]{:S(2)}) async-start(bf16[32,13,2048]{2,1,0:T(8,128)(2,1)} %copy.18), calls=%async_computation.1 | async-start | bytes 4194304 | tf_op jit(solution)/shard_map/all_to_all | solution.py:99
  634.3 88.4 %reduce-scatter.2.cloned.1.call-start = ((), (), s32[]{:S(2)}) async-start(), calls=%async_computation.6 | async-start | bytes 663552 | tf_op jit(solution)/shard_map/reduce_scatter | solution.py:103
Sparse Core Ops, SparseCore 0:
  9.9 99.4 all-gather.2
  112.0 94.9 all-gather.4
  455.1 99.8 all-reduce.2
  688.8 33.8 reduce-scatter.1
where the time goes:
time: 734 us; the launch traced here: 732 us
  waiting for transfers between devices  378 us (51%)
  starting transfers between devices  124 us (17%)
  matrix products  83.5 us (11%)
  blocking collectives  58.7 us (8%)
  other arithmetic  43.8 us (6%)
  local copies, waits for them, and re-layouts  30.9 us (4%)
  between operations  13.3 us (2%)
    ppermute x15, starting transfers between devices, from_behind(): lax.ppermute(value, axis, [(source, source + steps) for source in range(i...  118 us
    all_gather x1, waiting for transfers between devices, local(): lax.all_gather(w_in, 'expert', axis=1, tiled=True)  100 us
    psum x1, waiting for transfers between devices, spread(): return lax.psum(jnp.where(mine, shard, jnp.zeros_like(shard)), axis)  99.3 us
    all_gather x1, waiting for transfers between devices, local(): lax.all_gather(w_out, 'expert', axis=1, tiled=True)  97.6 us
    dot_general x8, matrix products, processor(): branch = jnp.dot(hidden, w_second, preferred_element_type=jnp.float32)  77.7 us
    all_to_all x1, blocking collectives, local(): lax.all_to_all(outgoing, 'expert', split_axis=0, concat_axis=0, tiled=True)  58.7 us
    all_to_all x1, waiting for transfers between devices, local(): lax.all_to_all(partial_value.astype(jnp.bfloat16), 'expert', split_axis=0...  46.3 us
    reduce_scatter x1, waiting for transfers between devices, local(): lax.psum_scatter((gate[:, None] * mine).astype(jnp.bfloat16), 'section',...  33 us
  transfers between devices with their start and end apart: 20, of which 5 were waited for; matrix products, arithmetic and copies ran while one was open for 4% of the time, Pallas kernels for 0%

commit v1 on v0

--- a/solution.py
+++ b/solution.py
@@ -12,7 +12,7 @@
 
 def spread(shard, axis, root):
     mine = lax.axis_index(axis) == root
-    return lax.psum(jnp.where(mine, shard, jnp.zeros_like(shard)), axis)
+    return jnp.sum(lax.all_gather(jnp.where(mine, shard, jnp.zeros_like(shard)), axis), axis=0)
 
 
 def normalize(rows):

time: 734 us -> 782 us (1.065)
  waiting for transfers between devices: 378 us -> 401 us
  other arithmetic: 43.8 us -> 58.6 us
    all_gather x0 -> x1, waiting for transfers between devices: none -> 123 us  [spread(): lax.all_gather(jnp.where(mine, shard, jnp.zeros_like(shard)), axis)]
    psum x1 -> x0, waiting for transfers between devices: 99.3 us -> none  [spread(): return lax.psum(jnp.where(mine, shard, jnp.zeros_like(shard)), axis)]
    reduce_sum x0 -> x1, other arithmetic: none -> 10.7 us  [spread(): jnp.sum(lax.all_gather(jnp.where(mine, shard, jnp.zeros_like(shard)), axi...]
where the time goes in v1:
time: 782 us; the launch traced here: 779 us
  waiting for transfers between devices  401 us (51%)
  starting transfers between devices  124 us (16%)
  matrix products  86.7 us (11%)
  blocking collectives  61.2 us (8%)
  other arithmetic  58.6 us (7%)
  local copies, waits for them, and re-layouts  34.7 us (4%)
  between operations  13.2 us (2%)
    all_gather x1, waiting for transfers between devices, spread(): lax.all_gather(jnp.where(mine, shard, jnp.zeros_like(shard)), axis)  123 us
    ppermute x15, starting transfers between devices, from_behind(): lax.ppermute(value, axis, [(source, source + steps) for source in range(i...  118 us
    all_gather x1, waiting for transfers between devices, local(): lax.all_gather(w_in, 'expert', axis=1, tiled=True)  101 us
    all_gather x1, waiting for transfers between devices, local(): lax.all_gather(w_out, 'expert', axis=1, tiled=True)  97.6 us
    dot_general x8, matrix products, processor(): branch = jnp.dot(hidden, w_second, preferred_element_type=jnp.float32)  77.7 us
    all_to_all x1, blocking collectives, local(): lax.all_to_all(outgoing, 'expert', split_axis=0, concat_axis=0, tiled=True)  61.2 us
    all_to_all x1, waiting for transfers between devices, local(): lax.all_to_all(partial_value.astype(jnp.bfloat16), 'expert', split_axis=0...  46.9 us
    reduce_scatter x1, waiting for transfers between devices, local(): lax.psum_scatter((gate[:, None] * mine).astype(jnp.bfloat16), 'section',...  30.4 us
  transfers between devices with their start and end apart: 20, of which 5 were waited for; matrix products, arithmetic and copies ran while one was open for 4% of the time, Pallas kernels for 0%

profile of v1, /device:TPU:8, one launch (start us, length us, event | category | flops | bytes accessed | tf_op | source)
XLA Modules:
  0.0 779.4 jit_solution(13329607932344686924)
XLA Ops:
  8.1 101.4 %all-gather.5.cloned.1.call-done = bf16[1,2048,2048]{2,1,0:T(8,128)(2,1)} async-done(((bf16[1,64,2048]{2,1,0:T(8,128)(2,1)}), bf16[1,2048,2048]{2,1,0:T(8,128)(2,1)}) %all-gather.5.cloned.1.call-update) | async-done | bytes 8388624 | tf_op jit(solution)/shard_map/all_gather | solution.py:38
  109.4 97.6 %all-gather.7.cloned.1.call-done = bf16[1,2048,2048]{2,1,0:T(8,128)(2,1)} async-done(((bf16[1,64,2048]{2,1,0:T(8,128)(2,1)}), bf16[1,2048,2048]{2,1,0:T(8,128)(2,1)}) %all-gather.7.cloned.1.call-update) | async-done | bytes 8388624 | tf_op jit(solution)/shard_map/all_gather | solution.py:39
  208.8 244.6 %while.16 = (s32[]{:T(128)}, bf16[72,2048]{1,0:T(8,128)(2,1)S(1)}, bf16[8,72,2048]{2,1,0:T(8,128)(2,1)}, s32[]{:T(128)}, pred[]{:T(512)}, /*index=5*/bf16[8,72,2...) while((s32[]{:T(128)}, bf16[72,2048]{1,0:T(8,128)(2,1)S(1)}, ...), condition=%wide.region_4.5_spmd, body=%wide.region_0.4_spmd.sunk | while | flops 1210613888 | bytes 21500040 | solution.py:65
  208.8 11.9 %conditional.2 = (bf16[72,2048]{1,0:T(8,128)(2,1)}, bf16[1,72,2048]{2,1,0:T(8,128)(2,1)S(1)}) conditional(s32[]{:T(128)} %convert_element_type.111, () %tuple.47, (pred[]{:T(512)}, bf16[8,72,2048]{2,1,0:T(8,128)(2,1)}, s32[]{:T(128)}, bf16[72,2048]{1,0:T(8,128)(2,1)S(1)}, bf16[2048,2048]{1,0:T(8,128)(2,1)}, ...), branch_computations={%region_1.1_spmd, %region_2.3_spmd} | conditional | flops 1210466432 | bytes 19434868 | solution.py:58
  210.0 9.7 %fusion = bf16[72,2048]{1,0:T(8,128)(2,1)} fusion(bf16[2048,2048]{1,0:T(8,128)(2,1)} %get-tuple-element.195, bf16[2048,2048]{1,0:T(8,128)(2,1)} %get-tuple-element.194, f32[72]{0:T(128)S(1)} %add_rsqrt_fusion, bf16[72,2048]{1,0:T(8,128)(2,1)S(1)} %get-tuple-element.193, bf16[8,72,2048]{2,1,0:T(8,128)(2,1)} %get-tuple-element.191, s32[]{:T(128)} %get-tuple-element.192, ...), kind=kOutput, calls=%fused_computation.4 | convolution fusion | flops 1209876480 | bytes 18254336 | tf_op jit(solution)/shard_map/while/body/eval_jaxpr/cond/branch_1_fun/dot_general | solution.py:29
  222.0 1.7 select_dynamic-update-slice_fusion.2
  223.7 11.8 %conditional.2 = (bf16[72,2048]{1,0:T(8,128)(2,1)}, bf16[1,72,2048]{2,1,0:T(8,128)(2,1)S(1)}) conditional(s32[]{:T(128)} %convert_element_type.111, () %tuple.47, (pred[]{:T(512)}, bf16[8,72,2048]{2,1,0:T(8,128)(2,1)}, s32[]{:T(128)}, bf16[72,2048]{1,0:T(8,128)(2,1)S(1)}, bf16[2048,2048]{1,0:T(8,128)(2,1)}, ...), branch_computations={%region_1.1_spmd, %region_2.3_spmd} | conditional | flops 1210466432 | bytes 19434868 | solution.py:58
  224.9 9.7 %fusion = bf16[72,2048]{1,0:T(8,128)(2,1)} fusion(bf16[2048,2048]{1,0:T(8,128)(2,1)} %get-tuple-element.195, bf16[2048,2048]{1,0:T(8,128)(2,1)} %get-tuple-element.194, f32[72]{0:T(128)S(1)} %add_rsqrt_fusion, bf16[72,2048]{1,0:T(8,128)(2,1)S(1)} %get-tuple-element.193, bf16[8,72,2048]{2,1,0:T(8,128)(2,1)} %get-tuple-element.191, s32[]{:T(128)} %get-tuple-element.192, ...), kind=kOutput, calls=%fused_computation.4 | convolution fusion | flops 1209876480 | bytes 18254336 | tf_op jit(solution)/shard_map/while/body/eval_jaxpr/cond/branch_1_fun/dot_general | solution.py:29
  235.6 1.9 collective-permute-start
  237.5 1.7 select_dynamic-update-slice_fusion.2
  239.2 11.8 %conditional.2 = (bf16[72,2048]{1,0:T(8,128)(2,1)}, bf16[1,72,2048]{2,1,0:T(8,128)(2,1)S(1)}) conditional(s32[]{:T(128)} %convert_element_type.111, () %tuple.47, (pred[]{:T(512)}, bf16[8,72,2048]{2,1,0:T(8,128)(2,1)}, s32[]{:T(128)}, bf16[72,2048]{1,0:T(8,128)(2,1)S(1)}, bf16[2048,2048]{1,0:T(8,128)(2,1)}, ...), branch_computations={%region_1.1_spmd, %region_2.3_spmd} | conditional | flops 1210466432 | bytes 19434868 | solution.py:58
  240.4 9.7 %fusion = bf16[72,2048]{1,0:T(8,128)(2,1)} fusion(bf16[2048,2048]{1,0:T(8,128)(2,1)} %get-tuple-element.195, bf16[2048,2048]{1,0:T(8,128)(2,1)} %get-tuple-element.194, f32[72]{0:T(128)S(1)} %add_rsqrt_fusion, bf16[72,2048]{1,0:T(8,128)(2,1)S(1)} %get-tuple-element.193, bf16[8,72,2048]{2,1,0:T(8,128)(2,1)} %get-tuple-element.191, s32[]{:T(128)} %get-tuple-element.192, ...), kind=kOutput, calls=%fused_computation.4 | convolution fusion | flops 1209876480 | bytes 18254336 | tf_op jit(solution)/shard_map/while/body/eval_jaxpr/cond/branch_1_fun/dot_general | solution.py:29
  251.1 4.1 collective-permute-start
  255.2 1.7 select_dynamic-update-slice_fusion.2
  257.0 11.8 %conditional.2 = (bf16[72,2048]{1,0:T(8,128)(2,1)}, bf16[1,72,2048]{2,1,0:T(8,128)(2,1)S(1)}) conditional(s32[]{:T(128)} %convert_element_type.111, () %tuple.47, (pred[]{:T(512)}, bf16[8,72,2048]{2,1,0:T(8,128)(2,1)}, s32[]{:T(128)}, bf16[72,2048]{1,0:T(8,128)(2,1)S(1)}, bf16[2048,2048]{1,0:T(8,128)(2,1)}, ...), branch_computations={%region_1.1_spmd, %region_2.3_spmd} | conditional | flops 1210466432 | bytes 19434868 | solution.py:58
  258.1 9.7 %fusion = bf16[72,2048]{1,0:T(8,128)(2,1)} fusion(bf16[2048,2048]{1,0:T(8,128)(2,1)} %get-tuple-element.195, bf16[2048,2048]{1,0:T(8,128)(2,1)} %get-tuple-element.194, f32[72]{0:T(128)S(1)} %add_rsqrt_fusion, bf16[72,2048]{1,0:T(8,128)(2,1)S(1)} %get-tuple-element.193, bf16[8,72,2048]{2,1,0:T(8,128)(2,1)} %get-tuple-element.191, s32[]{:T(128)} %get-tuple-element.192, ...), kind=kOutput, calls=%fused_computation.4 | convolution fusion | flops 1209876480 | bytes 18254336 | tf_op jit(solution)/shard_map/while/body/eval_jaxpr/cond/branch_1_fun/dot_general | solution.py:29
  268.8 6.5 collective-permute-start
  277.0 11.8 %conditional.2 = (bf16[72,2048]{1,0:T(8,128)(2,1)}, bf16[1,72,2048]{2,1,0:T(8,128)(2,1)S(1)}) conditional(s32[]{:T(128)} %convert_element_type.111, () %tuple.47, (pred[]{:T(512)}, bf16[8,72,2048]{2,1,0:T(8,128)(2,1)}, s32[]{:T(128)}, bf16[72,2048]{1,0:T(8,128)(2,1)S(1)}, bf16[2048,2048]{1,0:T(8,128)(2,1)}, ...), branch_computations={%region_1.1_spmd, %region_2.3_spmd} | conditional | flops 1210466432 | bytes 19434868 | solution.py:58
  278.2 9.7 %fusion = bf16[72,2048]{1,0:T(8,128)(2,1)} fusion(bf16[2048,2048]{1,0:T(8,128)(2,1)} %get-tuple-element.195, bf16[2048,2048]{1,0:T(8,128)(2,1)} %get-tuple-element.194, f32[72]{0:T(128)S(1)} %add_rsqrt_fusion, bf16[72,2048]{1,0:T(8,128)(2,1)S(1)} %get-tuple-element.193, bf16[8,72,2048]{2,1,0:T(8,128)(2,1)} %get-tuple-element.191, s32[]{:T(128)} %get-tuple-element.192, ...), kind=kOutput, calls=%fused_computation.4 | convolution fusion | flops 1209876480 | bytes 18254336 | tf_op jit(solution)/shard_map/while/body/eval_jaxpr/cond/branch_1_fun/dot_general | solution.py:29
  288.9 6.5 collective-permute-start
  295.4 1.8 select_dynamic-update-slice_fusion.2
  297.2 11.8 %conditional.2 = (bf16[72,2048]{1,0:T(8,128)(2,1)}, bf16[1,72,2048]{2,1,0:T(8,128)(2,1)S(1)}) conditional(s32[]{:T(128)} %convert_element_type.111, () %tuple.47, (pred[]{:T(512)}, bf16[8,72,2048]{2,1,0:T(8,128)(2,1)}, s32[]{:T(128)}, bf16[72,2048]{1,0:T(8,128)(2,1)S(1)}, bf16[2048,2048]{1,0:T(8,128)(2,1)}, ...), branch_computations={%region_1.1_spmd, %region_2.3_spmd} | conditional | flops 1210466432 | bytes 19434868 | solution.py:58
  298.3 9.7 %fusion = bf16[72,2048]{1,0:T(8,128)(2,1)} fusion(bf16[2048,2048]{1,0:T(8,128)(2,1)} %get-tuple-element.195, bf16[2048,2048]{1,0:T(8,128)(2,1)} %get-tuple-element.194, f32[72]{0:T(128)S(1)} %add_rsqrt_fusion, bf16[72,2048]{1,0:T(8,128)(2,1)S(1)} %get-tuple-element.193, bf16[8,72,2048]{2,1,0:T(8,128)(2,1)} %get-tuple-element.191, s32[]{:T(128)} %get-tuple-element.192, ...), kind=kOutput, calls=%fused_computation.4 | convolution fusion | flops 1209876480 | bytes 18254336 | tf_op jit(solution)/shard_map/while/body/eval_jaxpr/cond/branch_1_fun/dot_general | solution.py:29
  309.0 6.5 collective-permute-start
  315.5 1.8 select_dynamic-update-slice_fusion.2
  317.2 11.8 %conditional.2 = (bf16[72,2048]{1,0:T(8,128)(2,1)}, bf16[1,72,2048]{2,1,0:T(8,128)(2,1)S(1)}) conditional(s32[]{:T(128)} %convert_element_type.111, () %tuple.47, (pred[]{:T(512)}, bf16[8,72,2048]{2,1,0:T(8,128)(2,1)}, s32[]{:T(128)}, bf16[72,2048]{1,0:T(8,128)(2,1)S(1)}, bf16[2048,2048]{1,0:T(8,128)(2,1)}, ...), branch_computations={%region_1.1_spmd, %region_2.3_spmd} | conditional | flops 1210466432 | bytes 19434868 | solution.py:58
  318.4 9.7 %fusion = bf16[72,2048]{1,0:T(8,128)(2,1)} fusion(bf16[2048,2048]{1,0:T(8,128)(2,1)} %get-tuple-element.195, bf16[2048,2048]{1,0:T(8,128)(2,1)} %get-tuple-element.194, f32[72]{0:T(128)S(1)} %add_rsqrt_fusion, bf16[72,2048]{1,0:T(8,128)(2,1)S(1)} %get-tuple-element.193, bf16[8,72,2048]{2,1,0:T(8,128)(2,1)} %get-tuple-element.191, s32[]{:T(128)} %get-tuple-element.192, ...), kind=kOutput, calls=%fused_computation.4 | convolution fusion | flops 1209876480 | bytes 18254336 | tf_op jit(solution)/shard_map/while/body/eval_jaxpr/cond/branch_1_fun/dot_general | solution.py:29
  329.1 6.5 collective-permute-start
  335.6 1.8 select_dynamic-update-slice_fusion.2
  337.3 11.8 %conditional.2 = (bf16[72,2048]{1,0:T(8,128)(2,1)}, bf16[1,72,2048]{2,1,0:T(8,128)(2,1)S(1)}) conditional(s32[]{:T(128)} %convert_element_type.111, () %tuple.47, (pred[]{:T(512)}, bf16[8,72,2048]{2,1,0:T(8,128)(2,1)}, s32[]{:T(128)}, bf16[72,2048]{1,0:T(8,128)(2,1)S(1)}, bf16[2048,2048]{1,0:T(8,128)(2,1)}, ...), branch_computations={%region_1.1_spmd, %region_2.3_spmd} | conditional | flops 1210466432 | bytes 19434868 | solution.py:58
  338.5 9.7 %fusion = bf16[72,2048]{1,0:T(8,128)(2,1)} fusion(bf16[2048,2048]{1,0:T(8,128)(2,1)} %get-tuple-element.195, bf16[2048,2048]{1,0:T(8,128)(2,1)} %get-tuple-element.194, f32[72]{0:T(128)S(1)} %add_rsqrt_fusion, bf16[72,2048]{1,0:T(8,128)(2,1)S(1)} %get-tuple-element.193, bf16[8,72,2048]{2,1,0:T(8,128)(2,1)} %get-tuple-element.191, s32[]{:T(128)} %get-tuple-element.192, ...), kind=kOutput, calls=%fused_computation.4 | convolution fusion | flops 1209876480 | bytes 18254336 | tf_op jit(solution)/shard_map/while/body/eval_jaxpr/cond/branch_1_fun/dot_general | solution.py:29
  349.2 6.5 collective-permute-start
  355.7 1.8 select_dynamic-update-slice_fusion.2
  358.2 17.5 %collective-permute-start = (bf16[72,2048]{1,0:T(8,128)(2,1)}, bf16[72,2048]{1,0:T(8,128)(2,1)S(1)}, u32[]{:S(2)}, u32[]{:S(2)}) collective-permute-start(bf16[72,2048]{1,0:T(8,128)(2,1)} %get-tuple-element.287), channel_id=1, source_target_pairs={{0,32},{32,64},{64,96},{96,128},{128,160},{160,192},{192,224},{1,3... | collective-permute-start | bytes 884744 | tf_op jit(solution)/shard_map/while/body/eval_jaxpr/ppermute | solution.py:10
  375.8 1.8 select_dynamic-update-slice_fusion.2
  378.3 6.5 collective-permute-start
  384.8 1.8 select_dynamic-update-slice_fusion.2
  387.3 17.5 %collective-permute-start = (bf16[72,2048]{1,0:T(8,128)(2,1)}, bf16[72,2048]{1,0:T(8,128)(2,1)S(1)}, u32[]{:S(2)}, u32[]{:S(2)}) collective-permute-start(bf16[72,2048]{1,0:T(8,128)(2,1)} %get-tuple-element.287), channel_id=1, source_target_pairs={{0,32},{32,64},{64,96},{96,128},{128,160},{160,192},{192,224},{1,3... | collective-permute-start | bytes 884744 | tf_op jit(solution)/shard_map/while/body/eval_jaxpr/ppermute | solution.py:10
  404.9 1.8 select_dynamic-update-slice_fusion.2
  407.4 6.5 collective-permute-start
  413.9 1.8 select_dynamic-update-slice_fusion.2
  416.4 8.4 %collective-permute-start = (bf16[72,2048]{1,0:T(8,128)(2,1)}, bf16[72,2048]{1,0:T(8,128)(2,1)S(1)}, u32[]{:S(2)}, u32[]{:S(2)}) collective-permute-start(bf16[72,2048]{1,0:T(8,128)(2,1)} %get-tuple-element.287), channel_id=1, source_target_pairs={{0,32},{32,64},{64,96},{96,128},{128,160},{160,192},{192,224},{1,3... | collective-permute-start | bytes 884744 | tf_op jit(solution)/shard_map/while/body/eval_jaxpr/ppermute | solution.py:10
  424.9 1.8 select_dynamic-update-slice_fusion.2
  427.4 6.5 collective-permute-start
  433.9 1.8 select_dynamic-update-slice_fusion.2
  436.5 15.2 %collective-permute-start = (bf16[72,2048]{1,0:T(8,128)(2,1)}, bf16[72,2048]{1,0:T(8,128)(2,1)S(1)}, u32[]{:S(2)}, u32[]{:S(2)}) collective-permute-start(bf16[72,2048]{1,0:T(8,128)(2,1)} %get-tuple-element.287), channel_id=1, source_target_pairs={{0,32},{32,64},{64,96},{96,128},{128,160},{160,192},{192,224},{1,3... | collective-permute-start | bytes 884744 | tf_op jit(solution)/shard_map/while/body/eval_jaxpr/ppermute | solution.py:10
  451.6 1.8 select_dynamic-update-slice_fusion.2
  456.6 123.0 %all-gather.9.cloned.1.call-done = bf16[64,72,2048]{2,1,0:T(8,128)(2,1)} async-done(((bf16[8,72,2048]{2,1,0:T(8,128)(2,1)}), bf16[64,72,2048]{2,1,0:T(8,128)(2,1)}) %all-gather.9.cloned.1.call-update) | async-done | bytes 18874384 | tf_op jit(solution)/shard_map/all_gather | solution.py:15
  579.7 10.7 %reduce_sum.51 = bf16[8,72,2048]{2,1,0:T(8,128)(2,1)S(1)} reduce(bf16[8,8,72,2048]{3,2,1,0:T(8,128)(2,1)} %bitcast.49, bf16[]{:T(256)} %constant.118.clone.1), dimensions={0}, to_apply=%region_5.6 | reduce | flops 8257536 | bytes 21233666 | tf_op jit(solution)/shard_map/reduce_sum | solution.py:15
  590.4 1.8 gather_fusion
  593.6 3.0 convolution_convert_fusion.1
  596.6 2.8 reshape.75
  599.4 61.2 %all_to_all.10 = bf16[32,13,2048]{2,1,0:T(8,128)(2,1)} all-to-all(bf16[32,13,2048]{2,1,0:T(8,128)(2,1)} %reshape.75), channel_id=1, replica_groups=mesh['section'=8,'expert'=32] {'expert'}, dimensions={0} | all-to-all | bytes 3407872 | tf_op jit(solution)/shard_map/all_to_all | solution.py:89
  660.6 2.8 reshape.76
  663.4 3.0 multiply_convert_fusion.3
  669.7 2.3 copy.18
  672.0 5.6 all-to-all-start.1
  679.4 46.9 %all-to-all-done.1 = bf16[32,13,2048]{2,1,0:T(8,128)(2,1)} async-done(((bf16[32,13,2048]{2,1,0:T(8,128)(2,1)}), bf16[32,13,2048]{2,1,0:T(8,128)(2,1)}, u32[]{:S(2)}, u32[]{:S(2)}) %all-to-all-start.1) | async-done | bytes 1703968 | tf_op jit(solution)/shard_map/all_to_all | solution.py:99
  726.3 3.2 reshape.82
  729.5 4.5 gather_fusion.1
  734.0 2.3 multiply_convert_fusion.2
  737.1 30.4 %reduce-scatter.2.cloned.1.call-done = bf16[144,256]{1,0:T(8,128)(2,1)} async-done(((bf16[144,2048]{1,0:T(8,128)(2,1)}), bf16[144,256]{1,0:T(8,128)(2,1)}) %reduce-scatter.2.cloned.1.call-update) | async-done | bytes 73744 | tf_op jit(solution)/shard_map/reduce_scatter | solution.py:103
  767.6 3.5 scatter_custom_fusion
  771.0 1.8 convert_element_type.69
  (100 shorter events, 44.4 us)
Async XLA Ops:
  6.5 661.6 %copy-start = (bf16[1,256,2048]{2,1,0:T(8,128)(2,1)S(1)}, bf16[1,256,2048]{2,1,0:T(8,128)(2,1)}, u32[]{:S(2)}) copy-start(bf16[1,256,2048]{2,1,0:T(8,128)(2,1)} %param.17) | copy-start | bytes 3145732
  6.5 102.9 %all-gather.5.cloned.1.call-start = ((), (), s32[]{:S(2)}) async-start(), calls=%async_computation.3 | async-start | bytes 8650752 | tf_op jit(solution)/shard_map/all_gather | solution.py:38
  7.3 199.8 %all-gather.7.cloned.1.call-start = ((), (), s32[]{:S(2)}) async-start(), calls=%async_computation.4 | async-start | bytes 8650752 | tf_op jit(solution)/shard_map/all_gather | solution.py:39
  8.0 571.7 %all-gather.9.cloned.1.call-start = ((), (), s32[]{:S(2)}) async-start(), calls=%async_computation.6 | async-start | bytes 21233664 | tf_op jit(solution)/shard_map/all_gather | solution.py:15
  220.7 3.1 collective-permute-start
  235.6 3.7 collective-permute-start
  251.1 5.9 collective-permute-start
  268.8 8.2 %collective-permute-start = (bf16[72,2048]{1,0:T(8,128)(2,1)}, bf16[72,2048]{1,0:T(8,128)(2,1)S(1)}, u32[]{:S(2)}, u32[]{:S(2)}) collective-permute-start(bf16[72,2048]{1,0:T(8,128)(2,1)} %get-tuple-element.287), channel_id=1, source_target_pairs={{0,32},{32,64},{64,96},{96,128},{128,160},{160,192},{192,224},{1,3... | collective-permute-start | bytes 884744 | tf_op jit(solution)/shard_map/while/body/eval_jaxpr/ppermute | solution.py:10
  288.9 8.3 %collective-permute-start = (bf16[72,2048]{1,0:T(8,128)(2,1)}, bf16[72,2048]{1,0:T(8,128)(2,1)S(1)}, u32[]{:S(2)}, u32[]{:S(2)}) collective-permute-start(bf16[72,2048]{1,0:T(8,128)(2,1)} %get-tuple-element.287), channel_id=1, source_target_pairs={{0,32},{32,64},{64,96},{96,128},{128,160},{160,192},{192,224},{1,3... | collective-permute-start | bytes 884744 | tf_op jit(solution)/shard_map/while/body/eval_jaxpr/ppermute | solution.py:10
  309.0 8.2 %collective-permute-start = (bf16[72,2048]{1,0:T(8,128)(2,1)}, bf16[72,2048]{1,0:T(8,128)(2,1)S(1)}, u32[]{:S(2)}, u32[]{:S(2)}) collective-permute-start(bf16[72,2048]{1,0:T(8,128)(2,1)} %get-tuple-element.287), channel_id=1, source_target_pairs={{0,32},{32,64},{64,96},{96,128},{128,160},{160,192},{192,224},{1,3... | collective-permute-start | bytes 884744 | tf_op jit(solution)/shard_map/while/body/eval_jaxpr/ppermute | solution.py:10
  329.1 8.2 %collective-permute-start = (bf16[72,2048]{1,0:T(8,128)(2,1)}, bf16[72,2048]{1,0:T(8,128)(2,1)S(1)}, u32[]{:S(2)}, u32[]{:S(2)}) collective-permute-start(bf16[72,2048]{1,0:T(8,128)(2,1)} %get-tuple-element.287), channel_id=1, source_target_pairs={{0,32},{32,64},{64,96},{96,128},{128,160},{160,192},{192,224},{1,3... | collective-permute-start | bytes 884744 | tf_op jit(solution)/shard_map/while/body/eval_jaxpr/ppermute | solution.py:10
  349.2 8.2 %collective-permute-start = (bf16[72,2048]{1,0:T(8,128)(2,1)}, bf16[72,2048]{1,0:T(8,128)(2,1)S(1)}, u32[]{:S(2)}, u32[]{:S(2)}) collective-permute-start(bf16[72,2048]{1,0:T(8,128)(2,1)} %get-tuple-element.287), channel_id=1, source_target_pairs={{0,32},{32,64},{64,96},{96,128},{128,160},{160,192},{192,224},{1,3... | collective-permute-start | bytes 884744 | tf_op jit(solution)/shard_map/while/body/eval_jaxpr/ppermute | solution.py:10
  358.2 19.3 %collective-permute-start = (bf16[72,2048]{1,0:T(8,128)(2,1)}, bf16[72,2048]{1,0:T(8,128)(2,1)S(1)}, u32[]{:S(2)}, u32[]{:S(2)}) collective-permute-start(bf16[72,2048]{1,0:T(8,128)(2,1)} %get-tuple-element.287), channel_id=1, source_target_pairs={{0,32},{32,64},{64,96},{96,128},{128,160},{160,192},{192,224},{1,3... | collective-permute-start | bytes 884744 | tf_op jit(solution)/shard_map/while/body/eval_jaxpr/ppermute | solution.py:10
  378.3 8.3 %collective-permute-start = (bf16[72,2048]{1,0:T(8,128)(2,1)}, bf16[72,2048]{1,0:T(8,128)(2,1)S(1)}, u32[]{:S(2)}, u32[]{:S(2)}) collective-permute-start(bf16[72,2048]{1,0:T(8,128)(2,1)} %get-tuple-element.287), channel_id=1, source_target_pairs={{0,32},{32,64},{64,96},{96,128},{128,160},{160,192},{192,224},{1,3... | collective-permute-start | bytes 884744 | tf_op jit(solution)/shard_map/while/body/eval_jaxpr/ppermute | solution.py:10
  387.3 19.3 %collective-permute-start = (bf16[72,2048]{1,0:T(8,128)(2,1)}, bf16[72,2048]{1,0:T(8,128)(2,1)S(1)}, u32[]{:S(2)}, u32[]{:S(2)}) collective-permute-start(bf16[72,2048]{1,0:T(8,128)(2,1)} %get-tuple-element.287), channel_id=1, source_target_pairs={{0,32},{32,64},{64,96},{96,128},{128,160},{160,192},{192,224},{1,3... | collective-permute-start | bytes 884744 | tf_op jit(solution)/shard_map/while/body/eval_jaxpr/ppermute | solution.py:10
  407.4 8.3 %collective-permute-start = (bf16[72,2048]{1,0:T(8,128)(2,1)}, bf16[72,2048]{1,0:T(8,128)(2,1)S(1)}, u32[]{:S(2)}, u32[]{:S(2)}) collective-permute-start(bf16[72,2048]{1,0:T(8,128)(2,1)} %get-tuple-element.287), channel_id=1, source_target_pairs={{0,32},{32,64},{64,96},{96,128},{128,160},{160,192},{192,224},{1,3... | collective-permute-start | bytes 884744 | tf_op jit(solution)/shard_map/while/body/eval_jaxpr/ppermute | solution.py:10
  416.4 10.2 %collective-permute-start = (bf16[72,2048]{1,0:T(8,128)(2,1)}, bf16[72,2048]{1,0:T(8,128)(2,1)S(1)}, u32[]{:S(2)}, u32[]{:S(2)}) collective-permute-start(bf16[72,2048]{1,0:T(8,128)(2,1)} %get-tuple-element.287), channel_id=1, source_target_pairs={{0,32},{32,64},{64,96},{96,128},{128,160},{160,192},{192,224},{1,3... | collective-permute-start | bytes 884744 | tf_op jit(solution)/shard_map/while/body/eval_jaxpr/ppermute | solution.py:10
  427.4 8.3 %collective-permute-start = (bf16[72,2048]{1,0:T(8,128)(2,1)}, bf16[72,2048]{1,0:T(8,128)(2,1)S(1)}, u32[]{:S(2)}, u32[]{:S(2)}) collective-permute-start(bf16[72,2048]{1,0:T(8,128)(2,1)} %get-tuple-element.287), channel_id=1, source_target_pairs={{0,32},{32,64},{64,96},{96,128},{128,160},{160,192},{192,224},{1,3... | collective-permute-start | bytes 884744 | tf_op jit(solution)/shard_map/while/body/eval_jaxpr/ppermute | solution.py:10
  436.5 16.9 %collective-permute-start = (bf16[72,2048]{1,0:T(8,128)(2,1)}, bf16[72,2048]{1,0:T(8,128)(2,1)S(1)}, u32[]{:S(2)}, u32[]{:S(2)}) collective-permute-start(bf16[72,2048]{1,0:T(8,128)(2,1)} %get-tuple-element.287), channel_id=1, source_target_pairs={{0,32},{32,64},{64,96},{96,128},{128,160},{160,192},{192,224},{1,3... | collective-permute-start | bytes 884744 | tf_op jit(solution)/shard_map/while/body/eval_jaxpr/ppermute | solution.py:10
  455.0 0.7 copy-start.1
  455.0 1.5 copy-start.2
  672.0 54.2 %all-to-all-start.1 = ((bf16[32,13,2048]{2,1,0:T(8,128)(2,1)}), bf16[32,13,2048]{2,1,0:T(8,128)(2,1)}, u32[]{:S(2)}, u32[]{:S(2)}) async-start(bf16[32,13,2048]{2,1,0:T(8,128)(2,1)} %copy.18), calls=%async_computation.1 | async-start | bytes 4194304 | tf_op jit(solution)/shard_map/all_to_all | solution.py:99
  677.6 89.9 %reduce-scatter.2.cloned.1.call-start = ((), (), s32[]{:S(2)}) async-start(), calls=%async_computation.5 | async-start | bytes 663552 | tf_op jit(solution)/shard_map/reduce_scatter | solution.py:103
Sparse Core Ops, SparseCore 0:
  9.9 99.4 all-gather.4
  112.0 94.9 all-gather.6
  455.1 124.5 all-gather.8
  736.4 31.1 reduce-scatter.1
